TPU v7x, 512 devices: a whole 4x4x16 slice. The times are simulated.
512 devices in a mesh: dp: 64 (over z, y), fsdp: 8 (over x, core).
Axes of the slice: x: 4, y: 4, z: 16, core: 2. Of those that a mesh axis runs over, the one named last changes fastest.
Arguments:
- tokens: bfloat16 [65536, 2048], P('dp', 'fsdp'), may hold values from -6 to 6
- norm_gain: bfloat16 [2048], replicated, may hold values from 0.25 to 1.75
- query_gain: bfloat16 [128], replicated, as said below
- key_gain: bfloat16 [128], replicated, as said below
- w_query: bfloat16 [2048, 2048], P('dp', 'fsdp'), as said below
- w_key: bfloat16 [2048, 1024], P('dp', 'fsdp'), as said below
- w_value: bfloat16 [2048, 1024], P('dp', 'fsdp'), may hold values from -0.125 to 0.125
- w_out: bfloat16 [2048, 2048], P('dp', 'fsdp'), may hold values from -0.125 to 0.125
- prompt_lengths: int32 [64, 8], replicated, may hold values from 1 to 512, 1024 in all within a row
- span_group: int32 [64, 64], replicated, may hold values from 0 to 63, as said below
Outputs:
- attention_update: bfloat16 [65536, 2048], P('dp', 'fsdp')
- kv_cache: bfloat16 [65536, 8, 256], P('dp', 'fsdp')
Inputs may be any that keep to these rules, and one draw needn't show every extreme that they name: `prompt_lengths`: row g sums to 1024. `span_group`: row i names, in arrival order, the group of each of its 64 blocks of 16 rows; every group is named exactly 64 times in all; every row names exactly one group twice and leaves exactly one group out, and every group is the one named twice by exactly one row. `query_gain`: Positive. `key_gain`: Positive. `w_query`: entries of size about one over the square root of 2048. `w_key`: entries of size about one over the square root of 2048.
All inputs are finite; a program needn't handle non-finite values.
Results may differ from a plain program's by a relative error of at most 0.0075.
The roundings to bfloat16 on the way count: a program that leaves them out, or rounds other values in their place, can miss the bound.
Values may be sent and summed in bfloat16 or wider, within the bound.
No kernel may reach another device: no remote copies, remote signals or barrier semaphores. Data moves between devices by JAX's collectives and lax.ppermute only.
A program may use at most 64 MiB of HBM per device.

v0:
```python
import math
import jax
import jax.numpy as jnp
from jax import lax
from jax.sharding import Mesh, PartitionSpec as P

QH = 16
KVH = 8
HD = 128
DP = ("z_hi", "z_lo", "y")
epsilon = 1e-06
rope_base = 1000000.0


def for_sending(x):

    def short(part):
        return part.astype(jnp.bfloat16) if part.dtype == jnp.float32 else part

    return jax.tree.map(short, x)


def head_norm(inputs, gains):
    inv_rms = lax.rsqrt(jnp.mean(inputs * inputs, axis=-1, keepdims=True) + epsilon)
    return inputs * inv_rms * gains.astype(jnp.float32)


def rotate(inputs, offsets):
    half_dim = inputs.shape[-1] // 2
    frequency = jnp.power(
        rope_base, -2.0 * jnp.arange(half_dim, dtype=jnp.float32) / inputs.shape[-1]
    )
    angles = offsets.astype(jnp.float32)[:, None] * frequency[None, :]
    cosine = jnp.cos(angles)[:, None, :]
    sine_part = jnp.sin(angles)[:, None, :]
    first_half = inputs[..., :half_dim]
    second = inputs[..., half_dim:]
    return jnp.concatenate(
        [first_half * cosine - second * sine_part, second * cosine + first_half * sine_part],
        axis=-1,
    )


def prompt_layout(lengths, group_rows):
    prompt_end = jnp.cumsum(lengths)
    begins = prompt_end - lengths
    position = jnp.arange(group_rows, dtype=jnp.int32)
    inside = (position[:, None] >= begins[None, :]) & (position[:, None] < prompt_end[None, :])
    starts = jnp.sum(jnp.where(inside, begins[None, :], 0), axis=1)
    return (position, starts)


def attend(query_block, key_rot, value_rows, pos_block, start_block, position):
    scores = jnp.einsum(
        "qkrd,skd->krqs", query_block, key_rot, preferred_element_type=jnp.float32
    ) * (1.0 / math.sqrt(HD))
    allowed = (position[None, :] <= pos_block[:, None]) & (
        position[None, :] >= start_block[:, None]
    )
    masked = jnp.where(allowed[None, None], scores, -jnp.inf)
    row_max = jnp.max(masked, axis=-1, keepdims=True)
    exp_scores = jnp.exp(masked - row_max)
    probs = (exp_scores / jnp.sum(exp_scores, axis=-1, keepdims=True)).astype(jnp.bfloat16)
    return jnp.einsum(
        "krqs,skd->qkrd", probs, value_rows, preferred_element_type=jnp.float32
    ).astype(jnp.bfloat16)


def local(
    tokens,
    norm_gain,
    query_gain,
    key_gain,
    w_query,
    w_key,
    w_value,
    w_out,
    prompt_lengths,
    span_group,
):
    group_rows, width_local = tokens.shape
    groups = lax.axis_size(DP)
    arrival_rows = group_rows // groups
    device_index = lax.axis_index(DP)
    block_ids = jnp.arange(groups, dtype=jnp.int32)
    own_blocks = lax.dynamic_index_in_dim(span_group, device_index, 0, keepdims=False)
    same = own_blocks[:, None] == own_blocks[None, :]
    dup_rank = jnp.sum(same & (block_ids[None, :] < block_ids[:, None]), axis=1).astype(jnp.int32)
    first_dest = jnp.where(dup_rank == 0, own_blocks, groups)
    slot_source = jnp.zeros((groups,), jnp.int32).at[first_dest].set(block_ids, mode="drop")
    dup_block = jnp.sum(jnp.where(dup_rank == 1, block_ids, 0))
    token_blocks = tokens.reshape(groups, arrival_rows, width_local)
    dup_tokens = lax.dynamic_index_in_dim(token_blocks, dup_block, 0, keepdims=False)
    weights = jnp.concatenate([w_query, w_key, w_value, w_out], axis=1)
    weight_rows, weight_width = weights.shape
    packed = jnp.concatenate([weights, dup_tokens.reshape(weight_rows, -1)], axis=1)
    packed = lax.all_gather(packed, "y", axis=0, tiled=True)
    packed, token_blocks = lax.optimization_barrier((packed, token_blocks))
    packed = lax.all_gather(packed, "z_lo", axis=0, tiled=True)
    packed = lax.all_gather(packed, "z_hi", axis=0, tiled=True)
    weights = packed[:, :weight_width]
    dup_all = packed[:, weight_width:].reshape(groups, arrival_rows, width_local)
    outgoing = jnp.take(token_blocks, slot_source, axis=0, mode="clip")
    incoming = lax.all_to_all(outgoing, DP, split_axis=0, concat_axis=0, tiled=True)
    counts = jnp.sum((span_group == device_index).astype(jnp.int32), axis=1)
    offsets = jnp.cumsum(counts) - counts
    first_pos = jnp.where(counts >= 1, offsets, groups)
    second_pos = jnp.where(counts == 2, offsets + 1, groups)
    source_of = (
        jnp.zeros((groups,), jnp.int32)
        .at[first_pos]
        .set(block_ids, mode="drop")
        .at[second_pos]
        .set(block_ids + groups, mode="drop")
    )
    pool = jnp.concatenate([incoming, dup_all], axis=0)
    arrived = jnp.take(pool, source_of, axis=0, mode="clip").reshape(group_rows, width_local)
    arrived, weights = lax.optimization_barrier((arrived, weights))
    full_rows = lax.all_gather(arrived, "fsdp", axis=1, tiled=True)
    cuts = [w_query.shape[1], w_key.shape[1], w_value.shape[1], w_out.shape[1]]
    bounds = [sum(cuts[:k]) for k in range(5)]
    query_full, key_full, value_full, out_full = (
        weights[:, bounds[k] : bounds[k + 1]] for k in range(4)
    )
    lengths = lax.dynamic_index_in_dim(prompt_lengths, device_index, 0, keepdims=False)
    position, starts = prompt_layout(lengths, group_rows)
    within = position - starts
    floats = full_rows.astype(jnp.float32)
    normed = (
        floats
        * lax.rsqrt(jnp.mean(floats * floats, axis=-1, keepdims=True) + epsilon)
        * norm_gain.astype(jnp.float32)
    ).astype(jnp.bfloat16)
    query = jnp.dot(normed, query_full, preferred_element_type=jnp.float32).reshape(
        group_rows, -1, HD
    )
    key_rows = jnp.dot(normed, key_full, preferred_element_type=jnp.float32).reshape(
        group_rows, -1, HD
    )
    value_rows = (
        jnp.dot(normed, value_full, preferred_element_type=jnp.float32)
        .reshape(group_rows, -1, HD)
        .astype(jnp.bfloat16)
    )
    query_rot = rotate(head_norm(query, query_gain), within).astype(jnp.bfloat16)
    key_rot = rotate(head_norm(key_rows, key_gain), within).astype(jnp.bfloat16)
    kv_heads = key_rot.shape[1]
    group_ratio = QH // KVH
    cache_rows = jnp.concatenate([key_rot, value_rows], axis=-1)
    block_count = group_rows // 512
    block_len = group_rows // block_count
    query_heads = query_rot.reshape(block_count, block_len, kv_heads, group_ratio, HD)

    def one_block(pieces):
        query_block, pos_block, start_block = pieces
        return attend(query_block, key_rot, value_rows, pos_block, start_block, position)

    mixed = lax.map(
        one_block,
        (
            query_heads,
            position.reshape(block_count, block_len),
            starts.reshape(block_count, block_len),
        ),
    )
    mixed = mixed.reshape(group_rows, kv_heads * group_ratio * HD)
    heads_all = lax.all_gather(mixed, "fsdp", axis=1, tiled=True)
    update = jnp.dot(heads_all, out_full, preferred_element_type=jnp.float32).astype(jnp.bfloat16)
    cache_flat = cache_rows.reshape(group_rows, -1)
    update_width = update.shape[1]
    joined = jnp.concatenate([update, cache_flat], axis=1).reshape(groups, arrival_rows, -1)
    sent = jnp.take(joined, offsets, axis=0, mode="clip")
    dup_position = jnp.sum(jnp.where(counts == 2, offsets + 1, 0))
    dup_result = lax.dynamic_index_in_dim(joined, dup_position, 0, keepdims=True)
    dup_result = lax.all_gather(dup_result, "y", axis=0, tiled=True)
    dup_result = lax.all_gather(dup_result, "z_lo", axis=0, tiled=True)
    dup_result = lax.all_gather(dup_result, "z_hi", axis=0, tiled=True)
    back = lax.all_to_all(sent, DP, split_axis=0, concat_axis=0, tiled=True)
    pool_back = jnp.concatenate([back, dup_result], axis=0)
    mine = jnp.take(pool_back, own_blocks + groups * dup_rank, axis=0, mode="clip").reshape(
        group_rows, -1
    )
    attention_out = mine[:, :update_width]
    cache_out = mine[:, update_width:].reshape(cache_rows.shape)
    return (attention_out, cache_out)


def solution(mesh):
    z_size = mesh.shape["dp"] // 4
    fine = Mesh(
        mesh.devices.reshape(z_size // 4, 4, 4, mesh.shape["fsdp"]), ("z_hi", "z_lo", "y", "fsdp")
    )
    return jax.shard_map(
        local,
        mesh=fine,
        in_specs=(
            P(DP, "fsdp"),
            P(),
            P(),
            P(),
            P(DP, "fsdp"),
            P(DP, "fsdp"),
            P(DP, "fsdp"),
            P(DP, "fsdp"),
            P(),
            P(),
        ),
        out_specs=(P(DP, "fsdp"), P(DP, "fsdp", None)),
        check_vma=False,
    )
```

profile of v0, /device:TPU:1, one launch (start us, length us, event | category | flops | bytes accessed | tf_op | source)
XLA Modules:
  0.0 475.8 jit_solution(10181882392468857005)
XLA Ops:
  13.6 10.6 %all_gather.24 = bf16[128,896]{1,0:T(8,128)(2,1)S(1)} all-gather(bf16[32,896]{1,0:T(8,128)(2,1)S(1)} %constant_dynamic-update-slice_fusion), channel_id=1, replica_groups=mesh['z_hi'=4,'z_lo'=4,'y'=4,'fsdp'=8] {'y'}, dimensions={0}, use_global_device_ids=true | all-gather | bytes 286720 | tf_op jit(solution)/shard_map/all_gather | solution.py:97
  24.3 18.4 %all_gather.25 = bf16[512,896]{1,0:T(8,128)(2,1)} all-gather(bf16[128,896]{1,0:T(8,128)(2,1)S(1)} %all_gather.24), channel_id=1, replica_groups=mesh['z_hi'=4,'z_lo'=4,'y'=4,'fsdp'=8] {'z_lo'}, dimensions={0}, use_global_device_ids=true | all-gather | bytes 1146880 | tf_op jit(solution)/shard_map/all_gather | solution.py:99
  45.8 1.4 gather_fusion
  47.1 16.7 %all-to-all-start = ((bf16[64,16,256]{2,1,0:T(8,128)(2,1)}), bf16[64,16,256]{2,1,0:T(8,128)(2,1)S(1)}, u32[]{:S(2)}, u32[]{:S(2)}) async-start(bf16[64,16,256]{2,1,0:T(8,128)(2,1)} %gather_fusion), calls=%async_computation | async-start | bytes 1048576 | tf_op jit(solution)/shard_map/all_to_all | solution.py:104
  65.5 145.7 %all-gather.5.cloned.1.call-done = bf16[2048,896]{1,0:T(8,128)(2,1)} async-done(((bf16[512,896]{1,0:T(8,128)(2,1)}), bf16[2048,896]{1,0:T(8,128)(2,1)}) %all-gather.5.cloned.1.call-update) | async-done | bytes 3670032 | tf_op jit(solution)/shard_map/all_gather | solution.py:100
  211.2 1.1 slice.56
  212.7 1.4 gather_fusion.1
  214.1 3.8 slice.57
  219.4 37.9 %all-gather.7.cloned.1.call-done = bf16[1024,2048]{1,0:T(8,128)(2,1)} async-done(((bf16[1024,256]{1,0:T(8,128)(2,1)}), bf16[1024,2048]{1,0:T(8,128)(2,1)}) %all-gather.7.cloned.1.call-update) | async-done | bytes 4194320 | tf_op jit(solution)/shard_map/all_gather | solution.py:119
  257.3 3.2 fusion.21
  260.8 1.0 fusion.23
  262.7 1.5 multiply_reduce_fusion.1
  264.2 1.3 multiply_reduce_fusion
  265.5 1.2 convolution_convert_fusion.1
  266.9 1.3 fusion.35
  271.1 9.4 %while.12 = (s32[]{:T(128)}, bf16[2,512,1,2,128]{4,3,1,0,2:T(2,128)(2,1)S(1)}, s32[2,512]{1,0:T(2,128)S(1)}, s32[2,512]{1,0:T(2,128)S(1)}, bf16[2,512,1,2,128]{4...) while((s32[]{:T(128)}, ...), condition=%wide.region_15.16_spmd.clone.clone, body=%wide.region_12.15_spmd.clone.clone.sunk | while | flops 551155712 | bytes 16285793 | solution.py:158
  271.7 1.0 fusion.67
  272.8 1.2 fusion.68
  273.9 1.6 fusion.69
  276.4 1.0 fusion.67
  277.5 1.2 fusion.68
  278.7 1.6 fusion.69
  281.8 44.0 %all-gather.9.cloned.1.call-done = bf16[1024,2048]{1,0:T(8,128)(2,1)} async-done(((bf16[1024,256]{1,0:T(8,128)(2,1)}), bf16[1024,2048]{1,0:T(8,128)(2,1)}) %all-gather.9.cloned.1.call-update) | async-done | bytes 4194320 | tf_op jit(solution)/shard_map/all_gather | solution.py:167
  325.8 3.7 convolution_convert_fusion
  329.8 1.6 gather_fusion.2
  331.5 15.6 %all-to-all-start.1 = ((bf16[64,16,512]{2,1,0:T(8,128)(2,1)}), bf16[64,16,512]{2,1,0:T(8,128)(2,1)}, u32[]{:S(2)}, u32[]{:S(2)}) async-start(bf16[64,16,512]{2,1,0:T(8,128)(2,1)} %gather_fusion.2), calls=%async_computation.1 | async-start | bytes 2097152 | tf_op jit(solution)/shard_map/all_to_all | solution.py:178
  349.7 10.3 %all_gather.29 = bf16[4,16,512]{2,1,0:T(8,128)(2,1)S(1)} all-gather(bf16[1,16,512]{2,1,0:T(8,128)(2,1)S(1)} %constant_dynamic-slice_fusion.2), channel_id=1, replica_groups=mesh['z_hi'=4,'z_lo'=4,'y'=4,'fsdp'=8] {'y'}, dimensions={0}, use_global_device_ids=true | all-gather | bytes 81920 | tf_op jit(solution)/shard_map/all_gather | solution.py:175
  360.1 40.8 %all_gather.30 = bf16[16,16,512]{2,1,0:T(8,128)(2,1)} all-gather(bf16[4,16,512]{2,1,0:T(8,128)(2,1)S(1)} %all_gather.29), channel_id=1, replica_groups=mesh['z_hi'=4,'z_lo'=4,'y'=4,'fsdp'=8] {'z_lo'}, dimensions={0}, use_global_device_ids=true | all-gather | bytes 327680 | tf_op jit(solution)/shard_map/all_gather | solution.py:176
  400.9 62.8 %all-gather.11.cloned.1.call-done = bf16[64,16,512]{2,1,0:T(8,128)(2,1)} async-done(((bf16[16,16,512]{2,1,0:T(8,128)(2,1)}), bf16[64,16,512]{2,1,0:T(8,128)(2,1)}) %all-gather.11.cloned.1.call-update) | async-done | bytes 1048592 | tf_op jit(solution)/shard_map/all_gather | solution.py:177
  463.7 1.7 pad_maximum_fusion
  465.4 1.6 gather_fusion.3
  467.0 2.2 slice_bitcast_fusion
  (94 shorter events, 18.9 us)
Async XLA Ops:
  7.2 3.6 copy-start
  7.2 204.1 %all-gather.5.cloned.1.call-start = ((), (), s32[]{:S(2)}) async-start(), calls=%async_computation.2 | async-start | bytes 4587520 | tf_op jit(solution)/shard_map/all_gather | solution.py:100
  47.1 165.4 %all-to-all-start = ((bf16[64,16,256]{2,1,0:T(8,128)(2,1)}), bf16[64,16,256]{2,1,0:T(8,128)(2,1)S(1)}, u32[]{:S(2)}, u32[]{:S(2)}) async-start(bf16[64,16,256]{2,1,0:T(8,128)(2,1)} %gather_fusion), calls=%async_computation | async-start | bytes 1048576 | tf_op jit(solution)/shard_map/all_to_all | solution.py:104
  63.9 193.5 %all-gather.7.cloned.1.call-start = ((), (), s32[]{:S(2)}) async-start(), calls=%async_computation.3 | async-start | bytes 4718592 | tf_op jit(solution)/shard_map/all_gather | solution.py:119
  212.6 5.3 %copy-start.4 = (bf16[2048]{0:T(1024)(128)(2,1)S(1)}, bf16[2048]{0:T(1024)(128)(2,1)}, u32[]{:S(2)}) copy-start(bf16[2048]{0:T(1024)(128)(2,1)} %param.13) | copy-start | bytes 12292
  212.6 5.3 %copy-start.6 = (bf16[128]{0:T(256)(128)(2,1)S(1)}, bf16[128]{0:T(256)(128)(2,1)}, u32[]{:S(2)}) copy-start(bf16[128]{0:T(256)(128)(2,1)} %param.15) | copy-start | bytes 772
  212.6 5.3 %copy-start.5 = (s32[64,8]{0,1:T(8,128)S(1)}, s32[64,8]{0,1:T(8,128)}, u32[]{:S(2)}) copy-start(s32[64,8]{0,1:T(8,128)} %param.20) | copy-start | bytes 6148
  212.7 5.7 %copy-start.7 = (bf16[128]{0:T(256)(128)(2,1)S(1)}, bf16[128]{0:T(256)(128)(2,1)}, u32[]{:S(2)}) copy-start(bf16[128]{0:T(256)(128)(2,1)} %param.14) | copy-start | bytes 772
  217.8 107.9 %all-gather.9.cloned.1.call-start = ((), (), s32[]{:S(2)}) async-start(), calls=%async_computation.4 | async-start | bytes 4718592 | tf_op jit(solution)/shard_map/all_gather | solution.py:167
  257.3 3.4 copy-start.1
  260.8 1.9 copy-start.2
  269.3 1.7 copy-start.3
  331.5 132.2 %all-to-all-start.1 = ((bf16[64,16,512]{2,1,0:T(8,128)(2,1)}), bf16[64,16,512]{2,1,0:T(8,128)(2,1)}, u32[]{:S(2)}, u32[]{:S(2)}) async-start(bf16[64,16,512]{2,1,0:T(8,128)(2,1)} %gather_fusion.2), calls=%async_computation.1 | async-start | bytes 2097152 | tf_op jit(solution)/shard_map/all_to_all | solution.py:178
  347.1 116.6 %all-gather.11.cloned.1.call-start = ((), (), s32[]{:S(2)}) async-start(), calls=%async_computation.5 | async-start | bytes 1310720 | tf_op jit(solution)/shard_map/all_gather | solution.py:177
Sparse Core Ops, SparseCore 0:
  42.8 168.3 all-gather.4
  218.0 39.3 all-gather.6
  281.6 44.1 all-gather.8
  401.0 62.6 all-gather.10
where the time goes:
time: 477 us; the launch traced here: 476 us
  waiting for transfers between devices  290 us (61%)
  blocking collectives  80.1 us (17%)
  starting transfers between devices  32.5 us (7%)
  local copies, waits for them, and re-layouts  24.3 us (5%)
  between operations  18.1 us (4%)
  other arithmetic  17.1 us (4%)
  matrix products  13 us (3%)
    all_gather x1, waiting for transfers between devices, local(): packed = lax.all_gather(packed, 'z_hi', axis=0, tiled=True)  146 us
    all_gather x1, waiting for transfers between devices, local(): dup_result = lax.all_gather(dup_result, 'z_hi', axis=0, tiled=True)  62.8 us
    all_gather x1, waiting for transfers between devices, local(): heads_all = lax.all_gather(mixed, 'fsdp', axis=1, tiled=True)  44 us
    all_gather x1, blocking collectives, local(): dup_result = lax.all_gather(dup_result, 'z_lo', axis=0, tiled=True)  40.8 us
    all_gather x1, waiting for transfers between devices, local(): full_rows = lax.all_gather(arrived, 'fsdp', axis=1, tiled=True)  37.9 us
    all_gather x1, blocking collectives, local(): packed = lax.all_gather(packed, 'z_lo', axis=0, tiled=True)  18.4 us
    all_to_all x1, starting transfers between devices, local(): lax.all_to_all(outgoing, DP, split_axis=0, concat_axis=0, tiled=True)  16.7 us
    all_to_all x1, starting transfers between devices, local(): back = lax.all_to_all(sent, DP, split_axis=0, concat_axis=0, tiled=True)  15.6 us
  transfers between devices with their start and end apart: 6, of which 4 were waited for; matrix products, arithmetic and copies ran while one was open for 2% of the time, Pallas kernels for 0%

commit v1 on v0

--- a/solution.py
+++ b/solution.py
@@ -116,7 +116,10 @@
     pool = jnp.concatenate([incoming, dup_all], axis=0)
     arrived = jnp.take(pool, source_of, axis=0, mode="clip").reshape(group_rows, width_local)
     arrived, weights = lax.optimization_barrier((arrived, weights))
-    full_rows = lax.all_gather(arrived, "fsdp", axis=1, tiled=True)
+    full_rows = jnp.concatenate(
+        jax.lax.all_to_all(jnp.stack([arrived] * jax.lax.axis_size("fsdp"), axis=0), "fsdp", 0, 0),
+        axis=1,
+    )
     cuts = [w_query.shape[1], w_key.shape[1], w_value.shape[1], w_out.shape[1]]
     bounds = [sum(cuts[:k]) for k in range(5)]
     query_full, key_full, value_full, out_full = (

time: 477 us -> 495 us (1.038)
  local copies, waits for them, and re-layouts: 24.3 us -> 32.8 us
  starting transfers between devices: 32.5 us -> 38 us
    all_to_all x0 -> x1, waiting for transfers between devices: none -> 45.3 us  [local(): jax.lax.all_to_all(jnp.stack([arrived] * jax.lax.axis_size('fsdp'), axis=...]
    all_gather x1 -> x0, waiting for transfers between devices: 37.9 us -> none  [local(): full_rows = lax.all_gather(arrived, 'fsdp', axis=1, tiled=True)]
    all_gather x1, waiting for transfers between devices: 44 us -> 37.2 us  [local(): heads_all = lax.all_gather(mixed, 'fsdp', axis=1, tiled=True)]
    all_to_all x0 -> x1, local copies, waits for them, and re-layouts: none -> 6.45 us  [local(): jax.lax.all_to_all(jnp.stack([arrived] * jax.lax.axis_size('fsdp'), axis=...]
    all_to_all x0 -> x1, starting transfers between devices: none -> 5.63 us  [local(): jax.lax.all_to_all(jnp.stack([arrived] * jax.lax.axis_size('fsdp'), axis=...]
where the time goes in v1:
time: 495 us; the launch traced here: 493 us
  waiting for transfers between devices  291 us (59%)
  blocking collectives  80.1 us (16%)
  starting transfers between devices  38 us (8%)
  local copies, waits for them, and re-layouts  32.8 us (7%)
  between operations  18.1 us (4%)
  other arithmetic  17.7 us (4%)
  matrix products  15.1 us (3%)
    all_gather x1, waiting for transfers between devices, local(): packed = lax.all_gather(packed, 'z_hi', axis=0, tiled=True)  146 us
    all_gather x1, waiting for transfers between devices, local(): dup_result = lax.all_gather(dup_result, 'z_hi', axis=0, tiled=True)  62.8 us
    all_to_all x1, waiting for transfers between devices, local(): jax.lax.all_to_all(jnp.stack([arrived] * jax.lax.axis_size('fsdp'), axis=...  45.3 us
    all_gather x1, blocking collectives, local(): dup_result = lax.all_gather(dup_result, 'z_lo', axis=0, tiled=True)  40.8 us
    all_gather x1, waiting for transfers between devices, local(): heads_all = lax.all_gather(mixed, 'fsdp', axis=1, tiled=True)  37.2 us
    all_gather x1, blocking collectives, local(): packed = lax.all_gather(packed, 'z_lo', axis=0, tiled=True)  18.4 us
    all_to_all x1, starting transfers between devices, local(): lax.all_to_all(outgoing, DP, split_axis=0, concat_axis=0, tiled=True)  16.7 us
    all_to_all x1, starting transfers between devices, local(): back = lax.all_to_all(sent, DP, split_axis=0, concat_axis=0, tiled=True)  15.6 us
  transfers between devices with their start and end apart: 6, of which 4 were waited for; matrix products, arithmetic and copies ran while one was open for 2% of the time, Pallas kernels for 0%

profile of v1, /device:TPU:1, one launch (start us, length us, event | category | flops | bytes accessed | tf_op | source)
XLA Modules:
  0.0 493.3 jit_solution(6548145580259808417)
XLA Ops:
  13.6 10.6 %all_gather.21 = bf16[128,896]{1,0:T(8,128)(2,1)S(1)} all-gather(bf16[32,896]{1,0:T(8,128)(2,1)S(1)} %constant_dynamic-update-slice_fusion), channel_id=1, replica_groups=mesh['z_hi'=4,'z_lo'=4,'y'=4,'fsdp'=8] {'y'}, dimensions={0}, use_global_device_ids=true | all-gather | bytes 286720 | tf_op jit(solution)/shard_map/all_gather | solution.py:97
  24.3 18.4 %all_gather.22 = bf16[512,896]{1,0:T(8,128)(2,1)} all-gather(bf16[128,896]{1,0:T(8,128)(2,1)S(1)} %all_gather.21), channel_id=1, replica_groups=mesh['z_hi'=4,'z_lo'=4,'y'=4,'fsdp'=8] {'z_lo'}, dimensions={0}, use_global_device_ids=true | all-gather | bytes 1146880 | tf_op jit(solution)/shard_map/all_gather | solution.py:99
  45.8 1.4 gather_fusion
  47.1 16.7 %all-to-all-start = ((bf16[64,16,256]{2,1,0:T(8,128)(2,1)}), bf16[64,16,256]{2,1,0:T(8,128)(2,1)S(1)}, u32[]{:S(2)}, u32[]{:S(2)}) async-start(bf16[64,16,256]{2,1,0:T(8,128)(2,1)} %gather_fusion), calls=%async_computation | async-start | bytes 1048576 | tf_op jit(solution)/shard_map/all_to_all | solution.py:104
  65.5 145.8 %all-gather.4.cloned.1.call-done = bf16[2048,896]{1,0:T(8,128)(2,1)} async-done(((bf16[512,896]{1,0:T(8,128)(2,1)}), bf16[2048,896]{1,0:T(8,128)(2,1)}) %all-gather.4.cloned.1.call-update) | async-done | bytes 3670032 | tf_op jit(solution)/shard_map/all_gather | solution.py:100
  213.2 3.8 slice.57
  217.1 2.2 stack.2
  219.3 5.6 %all-to-all-start.1 = ((bf16[8,1024,256]{2,1,0:T(8,128)(2,1)}), bf16[8,1024,256]{2,1,0:T(8,128)(2,1)}, u32[]{:S(2)}, u32[]{:S(2)}) async-start(bf16[8,1024,256]{2,1,0:T(8,128)(2,1)} %stack.2), calls=%async_computation.1 | async-start | bytes 8388608 | tf_op jit(solution)/shard_map/all_to_all | solution.py:120
  226.5 1.3 slice_bitcast_fusion
  228.5 45.3 %all-to-all-done.1 = bf16[8,1024,256]{2,1,0:T(8,128)(2,1)} async-done(((bf16[8,1024,256]{2,1,0:T(8,128)(2,1)}), bf16[8,1024,256]{2,1,0:T(8,128)(2,1)}, u32[]{:S(2)}, u32[]{:S(2)}) %all-to-all-start.1) | async-done | bytes 4194336 | tf_op jit(solution)/shard_map/all_to_all | solution.py:120
  273.7 6.5 %copy.76 = bf16[8,1024,256]{1,2,0:T(8,128)(2,1)} copy(bf16[8,1024,256]{2,1,0:T(8,128)(2,1)} %all-to-all-done.1) | data formatting | bytes 8388608 | tf_op jit(solution)/shard_map/all_to_all | solution.py:120
  280.2 3.3 multiply_reduce_fusion
  284.7 3.0 convolution_convert_fusion.1
  287.7 1.9 multiply_reduce_fusion.2
  289.7 1.2 fusion.32
  290.9 1.1 multiply_convert_fusion
  292.0 1.3 multiply_reduce_fusion.1
  295.2 9.7 %while.12 = (s32[]{:T(128)}, bf16[2,512,1,2,128]{4,3,1,0,2:T(2,128)(2,1)S(1)}, s32[2,512]{1,0:T(2,128)S(1)}, s32[2,512]{1,0:T(2,128)S(1)}, bf16[2,512,1,2,128]{4...) while((s32[]{:T(128)}, ...), condition=%wide.region_15.16_spmd.clone.clone, body=%wide.region_12.15_spmd.clone.clone.sunk | while | flops 551155712 | bytes 17334404 | solution.py:161
  297.1 1.2 fusion.66
  298.2 1.6 fusion.67
  301.8 1.2 fusion.66
  303.0 1.6 fusion.67
  306.1 37.2 %all-gather.6.cloned.1.call-done = bf16[1024,2048]{1,0:T(8,128)(2,1)} async-done(((bf16[1024,256]{1,0:T(8,128)(2,1)}), bf16[1024,2048]{1,0:T(8,128)(2,1)}) %all-gather.6.cloned.1.call-update) | async-done | bytes 4194320 | tf_op jit(solution)/shard_map/all_gather | solution.py:170
  343.3 3.7 convolution_convert_fusion
  347.4 1.6 gather_fusion.2
  349.0 15.6 %all-to-all-start.2 = ((bf16[64,16,512]{2,1,0:T(8,128)(2,1)}), bf16[64,16,512]{2,1,0:T(8,128)(2,1)}, u32[]{:S(2)}, u32[]{:S(2)}) async-start(bf16[64,16,512]{2,1,0:T(8,128)(2,1)} %gather_fusion.2), calls=%async_computation.2 | async-start | bytes 2097152 | tf_op jit(solution)/shard_map/all_to_all | solution.py:181
  367.3 10.3 %all_gather.25 = bf16[4,16,512]{2,1,0:T(8,128)(2,1)S(1)} all-gather(bf16[1,16,512]{2,1,0:T(8,128)(2,1)S(1)} %constant_dynamic-slice_fusion.2), channel_id=1, replica_groups=mesh['z_hi'=4,'z_lo'=4,'y'=4,'fsdp'=8] {'y'}, dimensions={0}, use_global_device_ids=true | all-gather | bytes 81920 | tf_op jit(solution)/shard_map/all_gather | solution.py:178
  377.6 40.8 %all_gather.26 = bf16[16,16,512]{2,1,0:T(8,128)(2,1)} all-gather(bf16[4,16,512]{2,1,0:T(8,128)(2,1)S(1)} %all_gather.25), channel_id=1, replica_groups=mesh['z_hi'=4,'z_lo'=4,'y'=4,'fsdp'=8] {'z_lo'}, dimensions={0}, use_global_device_ids=true | all-gather | bytes 327680 | tf_op jit(solution)/shard_map/all_gather | solution.py:179
  418.5 62.8 %all-gather.8.cloned.1.call-done = bf16[64,16,512]{2,1,0:T(8,128)(2,1)} async-done(((bf16[16,16,512]{2,1,0:T(8,128)(2,1)}), bf16[64,16,512]{2,1,0:T(8,128)(2,1)}) %all-gather.8.cloned.1.call-update) | async-done | bytes 1048592 | tf_op jit(solution)/shard_map/all_gather | solution.py:180
  481.2 1.7 pad_maximum_fusion
  483.0 1.6 gather_fusion.3
  484.6 2.2 slice_bitcast_fusion.1
  (104 shorter events, 22.4 us)
Async XLA Ops:
  7.2 4.3 copy-start
  7.2 204.1 %all-gather.4.cloned.1.call-start = ((), (), s32[]{:S(2)}) async-start(), calls=%async_computation.3 | async-start | bytes 4587520 | tf_op jit(solution)/shard_map/all_gather | solution.py:100
  47.1 165.4 %all-to-all-start = ((bf16[64,16,256]{2,1,0:T(8,128)(2,1)}), bf16[64,16,256]{2,1,0:T(8,128)(2,1)S(1)}, u32[]{:S(2)}, u32[]{:S(2)}) async-start(bf16[64,16,256]{2,1,0:T(8,128)(2,1)} %gather_fusion), calls=%async_computation | async-start | bytes 1048576 | tf_op jit(solution)/shard_map/all_to_all | solution.py:104
  219.3 5.6 %copy-start.5 = (bf16[2048]{0:T(1024)(128)(2,1)S(1)}, bf16[2048]{0:T(1024)(128)(2,1)}, u32[]{:S(2)}) copy-start(bf16[2048]{0:T(1024)(128)(2,1)} %param.13) | copy-start | bytes 12292
  219.3 5.7 %copy-start.7 = (bf16[128]{0:T(256)(128)(2,1)S(1)}, bf16[128]{0:T(256)(128)(2,1)}, u32[]{:S(2)}) copy-start(bf16[128]{0:T(256)(128)(2,1)} %param.15) | copy-start | bytes 772
  219.3 5.7 %copy-start.6 = (s32[64,8]{0,1:T(8,128)S(1)}, s32[64,8]{0,1:T(8,128)}, u32[]{:S(2)}) copy-start(s32[64,8]{0,1:T(8,128)} %param.20) | copy-start | bytes 6148
  219.3 6.2 %copy-start.8 = (bf16[128]{0:T(256)(128)(2,1)S(1)}, bf16[128]{0:T(256)(128)(2,1)}, u32[]{:S(2)}) copy-start(bf16[128]{0:T(256)(128)(2,1)} %param.14) | copy-start | bytes 772
  219.3 54.4 %all-to-all-start.1 = ((bf16[8,1024,256]{2,1,0:T(8,128)(2,1)}), bf16[8,1024,256]{2,1,0:T(8,128)(2,1)}, u32[]{:S(2)}, u32[]{:S(2)}) async-start(bf16[8,1024,256]{2,1,0:T(8,128)(2,1)} %stack.2), calls=%async_computation.1 | async-start | bytes 8388608 | tf_op jit(solution)/shard_map/all_to_all | solution.py:120
  224.9 118.4 %all-gather.6.cloned.1.call-start = ((), (), s32[]{:S(2)}) async-start(), calls=%async_computation.4 | async-start | bytes 4718592 | tf_op jit(solution)/shard_map/all_gather | solution.py:170
  280.2 3.4 copy-start.1
  293.5 1.7 copy-start.2
  296.0 2.2 copy-start.3
  300.8 2.2 copy-start.3
  306.0 41.1 %copy-start.4 = (bf16[1024,1,128]{2,0,1:T(8,128)(2,1)S(1)}, bf16[1024,1,128]{2,0,1:T(8,128)(2,1)}, u32[]{:S(2)}) copy-start(bf16[1024,1,128]{2,0,1:T(8,128)(2,1)} %get-tuple-element.254) | copy-start | bytes 786436
  349.0 132.2 %all-to-all-start.2 = ((bf16[64,16,512]{2,1,0:T(8,128)(2,1)}), bf16[64,16,512]{2,1,0:T(8,128)(2,1)}, u32[]{:S(2)}, u32[]{:S(2)}) async-start(bf16[64,16,512]{2,1,0:T(8,128)(2,1)} %gather_fusion.2), calls=%async_computation.2 | async-start | bytes 2097152 | tf_op jit(solution)/shard_map/all_to_all | solution.py:181
  364.7 116.6 %all-gather.8.cloned.1.call-start = ((), (), s32[]{:S(2)}) async-start(), calls=%async_computation.5 | async-start | bytes 1310720 | tf_op jit(solution)/shard_map/all_gather | solution.py:180
Sparse Core Ops, SparseCore 0:
  42.8 168.3 all-gather.3
  305.9 37.4 all-gather.5
  418.6 62.6 all-gather.7
